TPU v7x, 256 devices: a whole 4x4x8 slice. The times are simulated.
256 devices in a mesh: expert: 16 (over x, y), dp: 16 (over z, core).
Axes of the slice: x: 4, y: 4, z: 8, core: 2. Of those that a mesh axis runs over, the one named last changes fastest.
Arguments:
- tokens: bfloat16 [4096, 4096], P(('expert', 'dp')), may hold values from -6 to 6
- grad_out: bfloat16 [4096, 4096], P(('expert', 'dp')), may hold values from -6 to 6
- gate_values: bfloat16 [4096, 2], P(('expert', 'dp')), may hold values from 0.099609375 to 1
- routes: int32 [4096, 2], P(('expert', 'dp')), may hold values from 0 to 31, all different within a row; in each aligned block of 16 rows (0 to 15, 16 to 31, ...) at most 2 rows name the same one
- gate_weight: bfloat16 [32, 1536, 4096], P('expert', 'dp'), may hold values from -0.09375 to 0.09375
- up_weight: bfloat16 [32, 1536, 4096], P('expert', 'dp'), may hold values from -0.09375 to 0.09375
- down_weight: bfloat16 [32, 1536, 4096], P('expert', 'dp'), may hold values from -0.15625 to 0.15625
Outputs:
- grad_tokens: bfloat16 [4096, 4096], P(('expert', 'dp'))
- grad_gates: float32 [4096, 2], P(('expert', 'dp'))
- grad_gate_weight: bfloat16 [32, 1536, 4096], P('expert', 'dp')
- grad_up_weight: bfloat16 [32, 1536, 4096], P('expert', 'dp')
- grad_down_weight: bfloat16 [32, 1536, 4096], P('expert', 'dp')
Inputs may be any that keep to these rules, and one draw needn't show every extreme that they name: `routes`: each row names 2 different experts. In each aligned block of 16 rows (the rows of one device) no expert is named by more than 2 rows, a bound that some block reaches.
All inputs are finite; a program needn't handle non-finite values.
Results may differ from a plain program's by a relative error of at most 0.019.
Values may be sent and summed in bfloat16 or wider, within the bound.
No kernel may reach another device: no remote copies, remote signals or barrier semaphores. Data moves between devices by JAX's collectives and lax.ppermute only.
A program may use at most 128 MiB of HBM per device.

v0:
```python
import jax
import jax.numpy as jnp
from jax import lax
from jax.sharding import PartitionSpec as P


def per_device(tokens, grad_out, gate_values, routes, gate_weight, up_weight, down_weight):
    tok_rows, model_width = tokens.shape
    chosen = routes.shape[1]
    local_experts = gate_weight.shape[0]
    groups = lax.axis_size("expert")
    replicas = lax.axis_size("dp")
    experts_all = local_experts * groups
    capacity = 2 * tok_rows * chosen // experts_all
    slot_count = experts_all * capacity
    flat_routes = routes.reshape(-1)
    onehot = (flat_routes[:, None] == jnp.arange(experts_all, dtype=jnp.int32)[None, :]).astype(
        jnp.int32
    )
    earlier = jnp.cumsum(onehot, axis=0) - onehot
    slot_rank = jnp.sum(earlier * onehot, axis=1)
    owner_col = flat_routes // local_experts
    local_id = flat_routes % local_experts
    slot_index = (local_id * groups + owner_col) * capacity + slot_rank
    placing = (jnp.arange(slot_count, dtype=jnp.int32)[:, None] == slot_index[None, :]).astype(
        jnp.float32
    )
    token_map = jnp.sum(placing.reshape(slot_count, tok_rows, chosen), axis=2).astype(jnp.bfloat16)
    slot_gates = jnp.dot(
        placing.astype(jnp.bfloat16), gate_values.reshape(-1), preferred_element_type=jnp.float32
    ).astype(jnp.bfloat16)
    x_slots = jnp.dot(token_map, tokens, preferred_element_type=jnp.float32).astype(jnp.bfloat16)
    dy_slots = jnp.dot(token_map, grad_out, preferred_element_type=jnp.float32).astype(jnp.bfloat16)
    block_shape = (local_experts, groups, capacity, model_width)
    arrived = (
        lax.all_to_all(
            x_slots.reshape(block_shape), "expert", split_axis=1, concat_axis=1, tiled=True
        ),
        lax.all_to_all(
            dy_slots.reshape(block_shape), "expert", split_axis=1, concat_axis=1, tiled=True
        ),
        lax.all_to_all(
            slot_gates.reshape(block_shape[:3]), "expert", split_axis=1, concat_axis=1, tiled=True
        ),
    )
    x_rows, dy_rows, gate_rows = (
        lax.all_gather(arrived[0], "dp", axis=2, tiled=True),
        lax.all_gather(arrived[1], "dp", axis=2, tiled=True),
        lax.all_gather(arrived[2], "dp", axis=2, tiled=True),
    )
    row_total = groups * replicas * capacity
    inputs = x_rows.reshape(local_experts, row_total, model_width)
    upstream = dy_rows.reshape(local_experts, row_total, model_width)
    weighting = gate_rows.reshape(local_experts, row_total).astype(jnp.float32)[..., None]
    gate_pre = jnp.einsum("lrd,lhd->lrh", inputs, gate_weight, preferred_element_type=jnp.float32)
    up_pre = jnp.einsum("lrd,lhd->lrh", inputs, up_weight, preferred_element_type=jnp.float32)
    back_hidden = jnp.einsum(
        "lrd,lhd->lrh", upstream, down_weight, preferred_element_type=jnp.float32
    )
    sigmoid_gate = jax.nn.sigmoid(gate_pre)
    activated = gate_pre * sigmoid_gate
    hidden = activated * up_pre
    gate_part = jnp.sum(back_hidden * hidden, axis=2)
    scaled = weighting * back_hidden
    grad_gate_pre = (
        scaled * up_pre * sigmoid_gate * (1.0 + gate_pre * (1.0 - sigmoid_gate))
    ).astype(jnp.bfloat16)
    grad_up_pre = (scaled * activated).astype(jnp.bfloat16)
    weighted_hidden = (weighting * hidden).astype(jnp.bfloat16)
    input_part = jnp.einsum(
        "lrh,lhd->lrd", grad_gate_pre, gate_weight, preferred_element_type=jnp.float32
    )
    input_part = input_part + jnp.einsum(
        "lrh,lhd->lrd", grad_up_pre, up_weight, preferred_element_type=jnp.float32
    )
    grad_gate_weight = jnp.einsum(
        "lrh,lrd->lhd", grad_gate_pre, inputs, preferred_element_type=jnp.float32
    ).astype(jnp.bfloat16)
    grad_up_weight = jnp.einsum(
        "lrh,lrd->lhd", grad_up_pre, inputs, preferred_element_type=jnp.float32
    ).astype(jnp.bfloat16)
    grad_down_weight = jnp.einsum(
        "lrh,lrd->lhd", weighted_hidden, upstream, preferred_element_type=jnp.float32
    ).astype(jnp.bfloat16)
    part_shape = (local_experts, groups, replicas * capacity, model_width)
    summed = lax.psum_scatter(
        input_part.reshape(part_shape).astype(jnp.bfloat16), "dp", scatter_dimension=2, tiled=True
    )
    returned = lax.all_to_all(summed, "expert", split_axis=1, concat_axis=1, tiled=True)
    returned = returned.reshape(slot_count, model_width)
    grad_tokens = lax.dot_general(
        token_map, returned, (((0,), (0,)), ((), ())), preferred_element_type=jnp.float32
    ).astype(jnp.bfloat16)
    gate_share = gate_part.reshape(local_experts, groups, replicas * capacity)
    gate_total = lax.psum(gate_share, "dp")
    own_gates = lax.dynamic_slice_in_dim(gate_total, lax.axis_index("dp") * capacity, capacity, 2)
    gate_back = lax.all_to_all(
        own_gates, "expert", split_axis=1, concat_axis=1, tiled=True
    ).reshape(slot_count)
    grad_gates = jnp.dot(gate_back, placing, precision=lax.Precision.HIGHEST).reshape(
        tok_rows, chosen
    )
    return (grad_tokens, grad_gates, grad_gate_weight, grad_up_weight, grad_down_weight)


def solution(mesh):
    return jax.shard_map(
        per_device,
        mesh=mesh,
        in_specs=(
            P(("expert", "dp"), None),
            P(("expert", "dp"), None),
            P(("expert", "dp"), None),
            P(("expert", "dp"), None),
            P("expert", "dp", None),
            P("expert", "dp", None),
            P("expert", "dp", None),
        ),
        out_specs=(
            P(("expert", "dp"), None),
            P(("expert", "dp"), None),
            P("expert", "dp", None),
            P("expert", "dp", None),
            P("expert", "dp", None),
        ),
        check_vma=False,
    )
```

profile of v0, /device:TPU:8, one launch (start us, length us, event | category | flops | bytes accessed | tf_op | source)
XLA Modules:
  0.0 287.3 jit_solution(16650401668262213078)
XLA Ops:
  7.2 0.9 copy.82
  8.8 1.2 convolution_convert_fusion.3
  10.4 0.5 copy.95
  10.8 17.3 %all_to_all.25 = bf16[2,16,2,4096]{3,2,0,1:T(2,128)(2,1)S(1)} all-to-all(bf16[2,16,2,4096]{3,2,0,1:T(2,128)(2,1)S(1)} %copy.95), channel_id=1, replica_groups=mesh['expert'=16,'dp'=16] {'expert'}, dimensions={1} | all-to-all | bytes 1048576 | tf_op jit(solution)/shard_map/all_to_all | solution.py:36
  28.2 1.1 copy.96
  29.3 1.2 convolution_convert_fusion.4
  31.4 13.7 %all_to_all.26 = bf16[2,16,2,4096]{3,2,0,1:T(2,128)(2,1)S(1)} all-to-all(bf16[2,16,2,4096]{3,2,0,1:T(2,128)(2,1)S(1)} %copy.92), channel_id=1, replica_groups=mesh['expert'=16,'dp'=16] {'expert'}, dimensions={1} | all-to-all | bytes 1048576 | tf_op jit(solution)/shard_map/all_to_all | solution.py:39
  45.0 1.1 copy.93
  46.7 10.8 %all_to_all.27 = bf16[2,16,2]{2,0,1:T(2,128)(2,1)S(1)} all-to-all(bf16[2,16,2]{2,0,1:T(2,128)(2,1)S(1)} %copy.89), channel_id=1, replica_groups=mesh['expert'=16,'dp'=16] {'expert'}, dimensions={1} | all-to-all | bytes 256 | tf_op jit(solution)/shard_map/all_to_all | solution.py:42
  57.6 20.6 %all_gather.9 = bf16[2,16,32]{1,0,2:T(2,128)(2,1)S(1)} all-gather(bf16[2,16,2]{1,0,2:T(2,128)(2,1)S(1)} %copy.90), channel_id=1, replica_groups=mesh['expert'=16,'dp'=16] {'dp'}, dimensions={2}, use_global_device_ids=true | all-gather | bytes 2176 | tf_op jit(solution)/shard_map/all_gather | solution.py:49
  78.4 7.3 %all-gather.5.cloned.1.call-done = bf16[2,16,32,4096]{3,1,0,2:T(8,128)(2,1)} async-done(((bf16[2,16,2,4096]{3,1,0,2:T(8,128)(2,1)}), bf16[2,16,32,4096]{3,1,0,2:T(8,128)(2,1)}) %all-gather.5.cloned.1.call-update) | async-done | bytes 8388624 | tf_op jit(solution)/shard_map/all_gather | solution.py:47
  85.7 11.2 %copy.97 = bf16[2,16,32,4096]{3,2,1,0:T(8,128)(2,1)} copy(bf16[2,16,32,4096]{3,1,0,2:T(8,128)(2,1)} %all-gather.5.cloned.1.call-done) | data formatting | bytes 16777216 | tf_op jit(solution)/shard_map/all_gather | solution.py:47
  96.9 6.6 %fusion.23 = f32[2,512,96]{1,2,0:T(8,128)S(1)} fusion(bf16[2,512,4096]{2,1,0:T(8,128)(2,1)} %bitcast.33, bf16[2,96,4096]{2,1,0:T(8,128)(2,1)S(1)} %copy-done), kind=kOutput, calls=%fused_computation.55 | convolution fusion | flops 805306368 | bytes 10354688 | tf_op jit(solution)/shard_map/lrd,lhd->lrh/dot_general | solution.py:55
  103.5 2.7 fusion.22
  106.2 36.3 %all-gather.3.cloned.1.call-done = bf16[2,16,32,4096]{3,1,0,2:T(8,128)(2,1)} async-done(((bf16[2,16,2,4096]{3,1,0,2:T(8,128)(2,1)}), bf16[2,16,32,4096]{3,1,0,2:T(8,128)(2,1)}) %all-gather.3.cloned.1.call-update) | async-done | bytes 8388624 | tf_op jit(solution)/shard_map/all_gather | solution.py:48
  142.5 11.5 %copy.94 = bf16[2,16,32,4096]{3,2,1,0:T(8,128)(2,1)} copy(bf16[2,16,32,4096]{3,1,0,2:T(8,128)(2,1)} %all-gather.3.cloned.1.call-done) | data formatting | bytes 16777216 | tf_op jit(solution)/shard_map/all_gather | solution.py:48
  154.0 6.2 %multiply_reduce_fusion = (f32[2,512]{1,0:T(2,128)S(1)}, bf16[2,512,96]{1,2,0:T(8,128)(2,1)S(1)}, bf16[2,512,96]{1,2,0:T(8,128)(2,1)S(1)}) fusion(f32[2,512,96]{1,2,0:T(8,128)S(1)} %fusion.22, f32[2,512,96]{1,2,0:T(8,128)S(1)} %fusion.23, f32[2,512]{1,0:T(2,128)S(1)} %reshape.148, bf16[2,512,4096]{2,1,0:T(8,128)(2,1)} %bitcast.37, ...), kind=kOutput, calls=%fused_computation.10 | convolution fusion | flops 806976512 | bytes 11149312 | tf_op jit(solution)/shard_map/lrd,lhd->lrh/dot_general | solution.py:57
  160.2 8.1 %fusion.24 = f32[2,512,4096]{2,1,0:T(8,128)} fusion(bf16[2,512,96]{1,2,0:T(8,128)(2,1)S(1)} %get-tuple-element.6, bf16[2,96,4096]{2,1,0:T(8,128)(2,1)S(1)} %copy-done), kind=kOutput, calls=%fused_computation.56 | convolution fusion | flops 805306368 | bytes 18546688 | tf_op jit(solution)/shard_map/lrh,lhd->lrd/dot_general | solution.py:70
  168.3 11.4 %add_convert_fusion = bf16[2,512,4096]{2,1,0:T(8,128)(2,1)} fusion(f32[2,512,4096]{2,1,0:T(8,128)} %fusion.24, bf16[2,512,96]{1,2,0:T(8,128)(2,1)S(1)} %get-tuple-element.7, bf16[2,96,4096]{2,1,0:T(8,128)(2,1)S(1)} %copy-done.4), kind=kOutput, calls=%fused_computation | convolution fusion | flops 813694976 | bytes 26935296 | tf_op jit(solution)/shard_map/lrh,lhd->lrd/dot_general | solution.py:73
  179.8 11.4 %copy.98 = bf16[2,16,32,4096]{3,1,0,2:T(8,128)(2,1)} copy(bf16[2,16,32,4096]{3,2,1,0:T(8,128)(2,1)} %bitcast.39) | data formatting | bytes 16777216 | tf_op jit(solution)/shard_map/convert_element_type | solution.py:87
  191.4 46.9 %psum.7 = f32[2,16,32]{2,1,0:T(8,128)S(1)} all-reduce(f32[2,16,32]{2,1,0:T(8,128)S(1)} %reshape.146), channel_id=1, replica_groups=mesh['expert'=16,'dp'=16] {'dp'}, use_global_device_ids=true, to_apply=%region_5.6 | all-reduce | flops 1024 | bytes 8192 | tf_op jit(solution)/shard_map/psum | solution.py:95
  238.4 0.6 copy.101
  239.0 7.3 %all-to-all-start.4 = ((f32[2,16,2]{2,0,1:T(2,128)}), f32[2,16,2]{2,0,1:T(2,128)S(1)}, u32[]{:S(2)}, u32[]{:S(2)}) async-start(f32[2,16,2]{2,0,1:T(2,128)} %copy.101), calls=%async_computation.5 | async-start | bytes 32768 | tf_op jit(solution)/shard_map/all_to_all | solution.py:97
  246.3 6.2 %convolution_convert_fusion = bf16[2,96,4096]{2,1,0:T(8,128)(2,1)} fusion(bf16[2,512,4096]{2,1,0:T(8,128)(2,1)} %bitcast.38, f32[2,512]{1,0:T(2,128)S(1)} %reshape.148, f32[2,512,96]{1,2,0:T(8,128)S(1)} %fusion.22, f32[2,512,96]{1,2,0:T(8,128)S(1)} %fusion.23), kind=kOutput, calls=%fused_computation.1 | convolution fusion | flops 806780928 | bytes 10752000 | tf_op jit(solution)/shard_map/lrh,lrd->lhd/dot_general | solution.py:82
  252.5 6.2 %convolution_convert_fusion.2 = bf16[2,96,4096]{2,1,0:T(8,128)(2,1)} fusion(bf16[2,512,96]{1,2,0:T(8,128)(2,1)S(1)} %get-tuple-element.6, bf16[2,512,4096]{2,1,0:T(8,128)(2,1)} %bitcast.34), kind=kOutput, calls=%fused_computation.3 | convolution fusion | flops 806092800 | bytes 10158080 | tf_op jit(solution)/shard_map/lrh,lrd->lhd/dot_general | solution.py:76
  258.6 2.4 reduce-scatter.2.cloned.1.call-done
  261.0 2.4 copy.99
  263.4 7.1 %all-to-all-start.3 = ((bf16[2,16,2,4096]{3,2,0,1:T(2,128)(2,1)}), bf16[2,16,2,4096]{3,2,0,1:T(2,128)(2,1)S(1)}, u32[]{:S(2)}, u32[]{:S(2)}) async-start(bf16[2,16,2,4096]{3,2,0,1:T(2,128)(2,1)} %copy.99), calls=%async_computation.4 | async-start | bytes 1048576 | tf_op jit(solution)/shard_map/all_to_all | solution.py:89
  270.5 6.1 %convolution_convert_fusion.1 = bf16[2,96,4096]{2,1,0:T(8,128)(2,1)} fusion(bf16[2,512,96]{1,2,0:T(8,128)(2,1)S(1)} %get-tuple-element.7, bf16[2,512,4096]{2,1,0:T(8,128)(2,1)} %bitcast.35), kind=kOutput, calls=%fused_computation.2 | convolution fusion | flops 806092800 | bytes 10158080 | tf_op jit(solution)/shard_map/lrh,lrd->lhd/dot_general | solution.py:79
  276.7 0.8 fusion.6
  277.5 1.8 all-to-all-done.3
  279.9 0.9 convolution_convert_fusion.5
  (49 shorter events, 3.8 us)
Async XLA Ops:
  7.2 89.7 %copy-start = (bf16[2,96,4096]{2,1,0:T(8,128)(2,1)S(1)}, bf16[2,96,4096]{2,1,0:T(8,128)(2,1)}, u32[]{:S(2)}) copy-start(bf16[2,96,4096]{2,1,0:T(8,128)(2,1)} %param.11) | copy-start | bytes 4718596
  7.2 39.0 %copy-start.6 = (bf16[16,2]{0,1:T(2,128)(2,1)S(1)}, bf16[16,2]{0,1:T(2,128)(2,1)}, u32[]{:S(2)}) copy-start(bf16[16,2]{0,1:T(2,128)(2,1)} %param.9) | copy-start | bytes 196
  7.2 78.5 %all-gather.5.cloned.1.call-start = ((), (), s32[]{:S(2)}) async-start(), calls=%async_computation.7 | async-start | bytes 8912896 | tf_op jit(solution)/shard_map/all_gather | solution.py:47
  29.3 113.3 %all-gather.3.cloned.1.call-start = ((), (), s32[]{:S(2)}) async-start(), calls=%async_computation.6 | async-start | bytes 8912896 | tf_op jit(solution)/shard_map/all_gather | solution.py:48
  46.1 214.9 %reduce-scatter.2.cloned.1.call-start = ((), (), s32[]{:S(2)}) async-start(), calls=%async_computation.8 | async-start | bytes 8912896 | tf_op jit(solution)/shard_map/reduce_scatter | solution.py:86
  96.9 6.6 %copy-start.2 = (bf16[2,16,32,4096]{3,2,1,0:T(8,128)(2,1)S(1)}, bf16[2,16,32,4096]{3,2,1,0:T(8,128)(2,1)}, u32[]{:S(2)}) copy-start(bf16[2,16,32,4096]{3,2,1,0:T(8,128)(2,1)} %copy.97) | copy-start | bytes 25165828
  96.9 6.6 %copy-start.3 = (bf16[2,96,4096]{2,1,0:T(8,128)(2,1)S(1)}, bf16[2,96,4096]{2,1,0:T(8,128)(2,1)}, u32[]{:S(2)}) copy-start(bf16[2,96,4096]{2,1,0:T(8,128)(2,1)} %param.12) | copy-start | bytes 4718596
  142.5 11.5 %copy-start.5 = (bf16[2,96,4096]{2,1,0:T(8,128)(2,1)S(1)}, bf16[2,96,4096]{2,1,0:T(8,128)(2,1)}, u32[]{:S(2)}) copy-start(bf16[2,96,4096]{2,1,0:T(8,128)(2,1)} %param.13) | copy-start | bytes 4718596
  160.2 8.1 %copy-start.4 = (bf16[2,96,4096]{2,1,0:T(8,128)(2,1)S(1)}, bf16[2,96,4096]{2,1,0:T(8,128)(2,1)}, u32[]{:S(2)}) copy-start(bf16[2,96,4096]{2,1,0:T(8,128)(2,1)} %param.12) | copy-start | bytes 4718596
  239.0 24.4 %all-to-all-start.4 = ((f32[2,16,2]{2,0,1:T(2,128)}), f32[2,16,2]{2,0,1:T(2,128)S(1)}, u32[]{:S(2)}, u32[]{:S(2)}) async-start(f32[2,16,2]{2,0,1:T(2,128)} %copy.101), calls=%async_computation.5 | async-start | bytes 32768 | tf_op jit(solution)/shard_map/all_to_all | solution.py:97
  263.4 15.8 %all-to-all-start.3 = ((bf16[2,16,2,4096]{3,2,0,1:T(2,128)(2,1)}), bf16[2,16,2,4096]{3,2,0,1:T(2,128)(2,1)S(1)}, u32[]{:S(2)}, u32[]{:S(2)}) async-start(bf16[2,16,2,4096]{3,2,0,1:T(2,128)(2,1)} %copy.99), calls=%async_computation.4 | async-start | bytes 1048576 | tf_op jit(solution)/shard_map/all_to_all | solution.py:89
  270.5 10.2 %copy-start.1 = (bf16[2,96,4096]{2,1,0:T(8,128)(2,1)S(1)}, bf16[2,96,4096]{2,1,0:T(8,128)(2,1)}, u32[]{:S(2)}) copy-start(bf16[2,96,4096]{2,1,0:T(8,128)(2,1)} %param.11) | copy-start | bytes 4718596
Sparse Core Ops, SparseCore 0:
  29.4 56.2 all-gather.4
  88.1 54.3 all-gather.2
  191.4 69.5 reduce-scatter.1
where the time goes:
time: 288 us; the launch traced here: 287 us
  blocking collectives  109 us (38%)
  matrix products  57.6 us (20%)
  waiting for transfers between devices  47.8 us (17%)
  local copies, waits for them, and re-layouts  43.6 us (15%)
  starting transfers between devices  14.5 us (5%)
  between operations  13.9 us (5%)
    psum x1, blocking collectives, per_device(): gate_total = lax.psum(gate_share, 'dp')  46.9 us
    all_gather x1, waiting for transfers between devices, per_device(): lax.all_gather(arrived[1], 'dp', axis=2, tiled=True)  36.3 us
    all_gather x1, blocking collectives, per_device(): lax.all_gather(arrived[2], 'dp', axis=2, tiled=True)  20.6 us
    all_to_all x1, blocking collectives, per_device(): lax.all_to_all(x_slots.reshape(block_shape), 'expert', split_axis=1, conc...  17.3 us
    all_to_all x1, blocking collectives, per_device(): lax.all_to_all(dy_slots.reshape(block_shape), 'expert', split_axis=1, con...  13.7 us
    all_gather x1, local copies, waits for them, and re-layouts, per_device(): lax.all_gather(arrived[1], 'dp', axis=2, tiled=True)  11.5 us
    convert_element_type x1, local copies, waits for them, and re-layouts, per_device(): input_part.reshape(part_shape).astype(jnp.bfloat16)  11.4 us
    dot_general x1, matrix products, per_device(): jnp.einsum('lrh,lhd->lrd', grad_up_pre, up_weight, preferred_element_type...  11.4 us
  transfers between devices with their start and end apart: 5, of which 4 were waited for; matrix products, arithmetic and copies ran while one was open for 16% of the time, Pallas kernels for 0%

commit v1 on v0

--- a/solution.py
+++ b/solution.py
@@ -44,7 +44,9 @@
         ),
     )
     x_rows, dy_rows, gate_rows = (
-        lax.all_gather(arrived[0], "dp", axis=2, tiled=True),
+        jnp.concatenate(
+            lax.all_to_all(jnp.stack([arrived[0]] * lax.axis_size("dp")), "dp", 0, 0), axis=2
+        ),
         lax.all_gather(arrived[1], "dp", axis=2, tiled=True),
         lax.all_gather(arrived[2], "dp", axis=2, tiled=True),
     )

time: 288 us -> 479 us (1.66)
  blocking collectives: 109 us -> 279 us
  waiting for transfers between devices: 47.8 us -> 23.7 us
  starting transfers between devices: 14.5 us -> 37.8 us
  local copies, waits for them, and re-layouts: 43.6 us -> 65.4 us
    all_gather x1, blocking collectives: 20.6 us -> 232 us  [per_device(): lax.all_gather(arrived[2], 'dp', axis=2, tiled=True)]
    all_to_all x3 -> x0, blocking collectives: 41.8 us -> none  [the longest x1 17.3 us: per_device(): lax.all_to_all(x_slots.reshape(block_shape), 'expert', split_axis=1, conc...]
    all_gather x1, waiting for transfers between devices: 36.3 us -> 0.02 us  [per_device(): lax.all_gather(arrived[1], 'dp', axis=2, tiled=True)]
    all_to_all x0 -> x4, starting transfers between devices: none -> 25.7 us  [the longest x1 8.62 us: per_device(): lax.all_to_all(jnp.stack([arrived[0]] * lax.axis_size('dp')), 'dp', 0, 0)]
    another operation x0 -> x2, local copies, waits for them, and re-layouts: none -> 21.7 us  [the longest x1 13.1 us: per_device(): inputs = x_rows.reshape(local_experts, row_total, model_width)]
    all_to_all x0 -> x4, waiting for transfers between devices: none -> 17.6 us  [the longest x1 8.37 us: per_device(): lax.all_to_all(dy_slots.reshape(block_shape), 'expert', split_axis=1, con...]
    all_gather x1 -> x0, local copies, waits for them, and re-layouts: 11.2 us -> none  [per_device(): lax.all_gather(arrived[0], 'dp', axis=2, tiled=True)]
    reshape x0 -> x1, local copies, waits for them, and re-layouts: none -> 9.45 us  [per_device(): jnp.concatenate(lax.all_to_all(jnp.stack([arrived[0]] * lax.axis_size('dp...]
  transfers between devices with their start and end apart: 5 -> 8, of which waited for: 4 -> 5; matrix products, arithmetic and copies ran while one was open for 16% -> 13% of each run, Pallas kernels for 0% -> 0%
where the time goes in v1:
time: 479 us; the launch traced here: 478 us
  blocking collectives  279 us (58%)
  local copies, waits for them, and re-layouts  65.4 us (14%)
  matrix products  57.5 us (12%)
  starting transfers between devices  37.8 us (8%)
  waiting for transfers between devices  23.7 us (5%)
  between operations  14.2 us (3%)
    all_gather x1, blocking collectives, per_device(): lax.all_gather(arrived[2], 'dp', axis=2, tiled=True)  232 us
    psum x1, blocking collectives, per_device(): gate_total = lax.psum(gate_share, 'dp')  46.2 us
    another operation x1, local copies, waits for them, and re-layouts, per_device(): inputs = x_rows.reshape(local_experts, row_total, model_width)  13.1 us
    dot_general x1, matrix products, per_device(): jnp.einsum('lrh,lhd->lrd', grad_up_pre, up_weight, preferred_element_type...  11.4 us
    all_gather x1, local copies, waits for them, and re-layouts, per_device(): lax.all_gather(arrived[1], 'dp', axis=2, tiled=True)  11.3 us
    convert_element_type x1, local copies, waits for them, and re-layouts, per_device(): input_part.reshape(part_shape).astype(jnp.bfloat16)  11.2 us
  transfers between devices with their start and end apart: 8, of which 5 were waited for; matrix products, arithmetic and copies ran while one was open for 13% of the time, Pallas kernels for 0%

profile of v1, /device:TPU:8, one launch (start us, length us, event | category | flops | bytes accessed | tf_op | source)
XLA Modules:
  0.0 477.8 jit_solution(17846363597377457881)
XLA Ops:
  10.2 7.4 %all-to-all-start = ((bf16[2,16,2]{2,0,1:T(2,128)(2,1)}), bf16[2,16,2]{2,0,1:T(2,128)(2,1)S(1)}, u32[]{:S(2)}, u32[]{:S(2)}) async-start(bf16[2,16,2]{2,0,1:T(2,128)(2,1)} %copy.89), calls=%async_computation | async-start | bytes 16384 | tf_op jit(solution)/shard_map/all_to_all | solution.py:42
  17.9 1.2 convolution_convert_fusion.3
  19.4 1.3 copy.95
  20.7 3.0 all-to-all-done
  23.7 4.8 %all-to-all-start.2 = ((bf16[2,16,2,4096]{3,2,0,1:T(2,128)(2,1)}), bf16[2,16,2,4096]{3,2,0,1:T(2,128)(2,1)S(1)}, u32[]{:S(2)}, u32[]{:S(2)}) async-start(bf16[2,16,2,4096]{3,2,0,1:T(2,128)(2,1)} %copy.95), calls=%async_computation.2 | async-start | bytes 1048576 | tf_op jit(solution)/shard_map/all_to_all | solution.py:36
  28.6 1.2 convolution_convert_fusion.4
  30.1 1.3 copy.92
  31.4 6.2 %all-to-all-done.2 = bf16[2,16,2,4096]{3,2,0,1:T(2,128)(2,1)S(1)} async-done(((bf16[2,16,2,4096]{3,2,0,1:T(2,128)(2,1)}), bf16[2,16,2,4096]{3,2,0,1:T(2,128)(2,1)S(1)}, u32[]{:S(2)}, u32[]{:S(2)}) %all-to-all-start.2) | async-done | bytes 524320 | tf_op jit(solution)/shard_map/all_to_all | solution.py:36
  37.6 4.8 %all-to-all-start.1 = ((bf16[2,16,2,4096]{3,2,0,1:T(2,128)(2,1)}), bf16[2,16,2,4096]{3,2,0,1:T(2,128)(2,1)S(1)}, u32[]{:S(2)}, u32[]{:S(2)}) async-start(bf16[2,16,2,4096]{3,2,0,1:T(2,128)(2,1)} %copy.92), calls=%async_computation.1 | async-start | bytes 1048576 | tf_op jit(solution)/shard_map/all_to_all | solution.py:39
  42.9 8.4 %all-to-all-done.1 = bf16[2,16,2,4096]{3,2,0,1:T(2,128)(2,1)S(1)} async-done(((bf16[2,16,2,4096]{3,2,0,1:T(2,128)(2,1)}), bf16[2,16,2,4096]{3,2,0,1:T(2,128)(2,1)S(1)}, u32[]{:S(2)}, u32[]{:S(2)}) %all-to-all-start.1) | async-done | bytes 524320 | tf_op jit(solution)/shard_map/all_to_all | solution.py:39
  51.3 8.6 %stack.2 = bf16[16,2,16,2,4096]{4,3,2,1,0:T(2,128)(2,1)} broadcast(bf16[2,16,2,4096]{3,2,1,0:T(2,128)(2,1)S(1)} %copy.96), dimensions={1,2,3,4} | broadcast | bytes 8912896 | tf_op jit(solution)/shard_map/stack | solution.py:48
  59.8 8.6 %all-to-all-start.3 = ((bf16[16,2,16,2,4096]{4,3,2,1,0:T(2,128)(2,1)}), bf16[16,2,16,2,4096]{4,3,2,1,0:T(2,128)(2,1)}, u32[]{:S(2)}, u32[]{:S(2)}) async-start(bf16[16,2,16,2,4096]{4,3,2,1,0:T(2,128)(2,1)} %stack.2), calls=%async_computation.3 | async-start | bytes 16777216 | tf_op jit(solution)/shard_map/all_to_all | solution.py:48
  68.5 1.1 copy.93
  69.8 232.4 %all_gather.6 = bf16[2,16,32]{1,0,2:T(2,128)(2,1)S(1)} all-gather(bf16[2,16,2]{1,0,2:T(2,128)(2,1)S(1)} %copy.90), channel_id=1, replica_groups=mesh['expert'=16,'dp'=16] {'dp'}, dimensions={2}, use_global_device_ids=true | all-gather | bytes 2176 | tf_op jit(solution)/shard_map/all_gather | solution.py:51
  302.3 9.4 %copy.97 = bf16[2,16,16,2,4096]{4,3,2,1,0:T(2,128)(2,1)} copy(bf16[2,16,16,2,4096]{4,3,1,0,2:T(2,128)(2,1)} %bitcast.2) | data formatting | bytes 16777216 | tf_op jit(solution)/shard_map/reshape | solution.py:47
  311.8 13.1 %reshape_reshape.3 = bf16[2,512,4096]{2,1,0:T(8,128)(2,1)} reshape(bf16[2,16,16,2,4096]{4,3,2,1,0:T(2,128)(2,1)} %copy.97) | data formatting | bytes 16777216 | tf_op jit(solution)/shard_map/reshape;reshape | solution.py:54
  324.9 6.2 %fusion.23 = f32[2,512,96]{1,2,0:T(8,128)S(1)} fusion(bf16[2,512,4096]{2,1,0:T(8,128)(2,1)} %reshape_reshape.3, bf16[2,96,4096]{2,1,0:T(8,128)(2,1)S(1)} %copy-done), kind=kOutput, calls=%fused_computation.55 | convolution fusion | flops 805306368 | bytes 10354688 | tf_op jit(solution)/shard_map/lrd,lhd->lrh/dot_general | solution.py:57
  331.2 2.7 fusion.22
  333.9 11.3 %copy.94 = bf16[2,16,32,4096]{3,2,1,0:T(8,128)(2,1)} copy(bf16[2,16,32,4096]{3,1,0,2:T(8,128)(2,1)} %all-gather.2.cloned.1.call-done) | data formatting | bytes 16777216 | tf_op jit(solution)/shard_map/all_gather | solution.py:50
  345.2 6.2 %multiply_reduce_fusion = (f32[2,512]{1,0:T(2,128)S(1)}, bf16[2,512,96]{1,2,0:T(8,128)(2,1)S(1)}, bf16[2,512,96]{1,2,0:T(8,128)(2,1)S(1)}) fusion(f32[2,512,96]{1,2,0:T(8,128)S(1)} %fusion.22, f32[2,512,96]{1,2,0:T(8,128)S(1)} %fusion.23, f32[2,512]{1,0:T(2,128)S(1)} %reshape.150, bf16[2,512,4096]{2,1,0:T(8,128)(2,1)} %bitcast.33, ...), kind=kOutput, calls=%fused_computation.10 | convolution fusion | flops 806976512 | bytes 11149312 | tf_op jit(solution)/shard_map/lrd,lhd->lrh/dot_general | solution.py:59
  351.4 8.3 %fusion.24 = f32[2,512,4096]{2,1,0:T(8,128)} fusion(bf16[2,512,96]{1,2,0:T(8,128)(2,1)S(1)} %get-tuple-element.6, bf16[2,96,4096]{2,1,0:T(8,128)(2,1)S(1)} %copy-done), kind=kOutput, calls=%fused_computation.56 | convolution fusion | flops 805306368 | bytes 18546688 | tf_op jit(solution)/shard_map/lrh,lhd->lrd/dot_general | solution.py:72
  359.8 11.4 %add_convert_fusion = bf16[2,512,4096]{2,1,0:T(8,128)(2,1)} fusion(f32[2,512,4096]{2,1,0:T(8,128)} %fusion.24, bf16[2,512,96]{1,2,0:T(8,128)(2,1)S(1)} %get-tuple-element.7, bf16[2,96,4096]{2,1,0:T(8,128)(2,1)S(1)} %copy-done.4), kind=kOutput, calls=%fused_computation | convolution fusion | flops 813694976 | bytes 26935296 | tf_op jit(solution)/shard_map/lrh,lhd->lrd/dot_general | solution.py:75
  371.2 11.2 %copy.98 = bf16[2,16,32,4096]{3,1,0,2:T(8,128)(2,1)} copy(bf16[2,16,32,4096]{3,2,1,0:T(8,128)(2,1)} %bitcast.35) | data formatting | bytes 16777216 | tf_op jit(solution)/shard_map/convert_element_type | solution.py:89
  382.6 46.2 %psum.7 = f32[2,16,32]{2,1,0:T(8,128)S(1)} all-reduce(f32[2,16,32]{2,1,0:T(8,128)S(1)} %reshape.148), channel_id=1, replica_groups=mesh['expert'=16,'dp'=16] {'dp'}, use_global_device_ids=true, to_apply=%region_5.6 | all-reduce | flops 1024 | bytes 8192 | tf_op jit(solution)/shard_map/psum | solution.py:97
  429.6 5.0 %all-to-all-start.5 = ((f32[2,16,2]{2,0,1:T(2,128)}), f32[2,16,2]{2,0,1:T(2,128)S(1)}, u32[]{:S(2)}, u32[]{:S(2)}) async-start(f32[2,16,2]{2,0,1:T(2,128)} %copy.101), calls=%async_computation.6 | async-start | bytes 32768 | tf_op jit(solution)/shard_map/all_to_all | solution.py:99
  434.6 6.2 %convolution_convert_fusion = bf16[2,96,4096]{2,1,0:T(8,128)(2,1)} fusion(bf16[2,512,4096]{2,1,0:T(8,128)(2,1)} %bitcast.34, f32[2,512]{1,0:T(2,128)S(1)} %reshape.150, f32[2,512,96]{1,2,0:T(8,128)S(1)} %fusion.22, f32[2,512,96]{1,2,0:T(8,128)S(1)} %fusion.23), kind=kOutput, calls=%fused_computation.1 | convolution fusion | flops 806780928 | bytes 10752000 | tf_op jit(solution)/shard_map/lrh,lrd->lhd/dot_general | solution.py:84
  440.8 6.2 %convolution_convert_fusion.2 = bf16[2,96,4096]{2,1,0:T(8,128)(2,1)} fusion(bf16[2,512,96]{1,2,0:T(8,128)(2,1)S(1)} %get-tuple-element.6, bf16[2,512,4096]{2,1,0:T(8,128)(2,1)} %reshape_reshape.3), kind=kOutput, calls=%fused_computation.3 | convolution fusion | flops 806092800 | bytes 10158080 | tf_op jit(solution)/shard_map/lrh,lrd->lhd/dot_general | solution.py:78
  446.9 4.3 reduce-scatter.2.cloned.1.call-done
  451.2 2.4 copy.99
  453.6 7.1 %all-to-all-start.4 = ((bf16[2,16,2,4096]{3,2,0,1:T(2,128)(2,1)}), bf16[2,16,2,4096]{3,2,0,1:T(2,128)(2,1)S(1)}, u32[]{:S(2)}, u32[]{:S(2)}) async-start(bf16[2,16,2,4096]{3,2,0,1:T(2,128)(2,1)} %copy.99), calls=%async_computation.5 | async-start | bytes 1048576 | tf_op jit(solution)/shard_map/all_to_all | solution.py:91
  460.7 6.1 %convolution_convert_fusion.1 = bf16[2,96,4096]{2,1,0:T(8,128)(2,1)} fusion(bf16[2,512,96]{1,2,0:T(8,128)(2,1)S(1)} %get-tuple-element.7, bf16[2,512,4096]{2,1,0:T(8,128)(2,1)} %reshape_reshape.3), kind=kOutput, calls=%fused_computation.2 | convolution fusion | flops 806092800 | bytes 10158080 | tf_op jit(solution)/shard_map/lrh,lrd->lhd/dot_general | solution.py:81
  467.7 1.8 all-to-all-done.4
  (51 shorter events, 8.0 us)
Async XLA Ops:
  7.2 317.7 %copy-start = (bf16[2,96,4096]{2,1,0:T(8,128)(2,1)S(1)}, bf16[2,96,4096]{2,1,0:T(8,128)(2,1)}, u32[]{:S(2)}) copy-start(bf16[2,96,4096]{2,1,0:T(8,128)(2,1)} %param.11) | copy-start | bytes 4718596
  10.2 13.5 %all-to-all-start = ((bf16[2,16,2]{2,0,1:T(2,128)(2,1)}), bf16[2,16,2]{2,0,1:T(2,128)(2,1)S(1)}, u32[]{:S(2)}, u32[]{:S(2)}) async-start(bf16[2,16,2]{2,0,1:T(2,128)(2,1)} %copy.89), calls=%async_computation | async-start | bytes 16384 | tf_op jit(solution)/shard_map/all_to_all | solution.py:42
  23.7 13.9 %all-to-all-start.2 = ((bf16[2,16,2,4096]{3,2,0,1:T(2,128)(2,1)}), bf16[2,16,2,4096]{3,2,0,1:T(2,128)(2,1)S(1)}, u32[]{:S(2)}, u32[]{:S(2)}) async-start(bf16[2,16,2,4096]{3,2,0,1:T(2,128)(2,1)} %copy.95), calls=%async_computation.2 | async-start | bytes 1048576 | tf_op jit(solution)/shard_map/all_to_all | solution.py:36
  37.6 13.6 %all-to-all-start.1 = ((bf16[2,16,2,4096]{3,2,0,1:T(2,128)(2,1)}), bf16[2,16,2,4096]{3,2,0,1:T(2,128)(2,1)S(1)}, u32[]{:S(2)}, u32[]{:S(2)}) async-start(bf16[2,16,2,4096]{3,2,0,1:T(2,128)(2,1)} %copy.92), calls=%async_computation.1 | async-start | bytes 1048576 | tf_op jit(solution)/shard_map/all_to_all | solution.py:39
  59.8 242.5 %all-to-all-start.3 = ((bf16[16,2,16,2,4096]{4,3,2,1,0:T(2,128)(2,1)}), bf16[16,2,16,2,4096]{4,3,2,1,0:T(2,128)(2,1)}, u32[]{:S(2)}, u32[]{:S(2)}) async-start(bf16[16,2,16,2,4096]{4,3,2,1,0:T(2,128)(2,1)} %stack.2), calls=%async_computation.3 | async-start | bytes 16777216 | tf_op jit(solution)/shard_map/all_to_all | solution.py:48
  68.5 265.4 %all-gather.2.cloned.1.call-start = ((), (), s32[]{:S(2)}) async-start(), calls=%async_computation.7 | async-start | bytes 8912896 | tf_op jit(solution)/shard_map/all_gather | solution.py:50
  69.6 381.6 %reduce-scatter.2.cloned.1.call-start = ((), (), s32[]{:S(2)}) async-start(), calls=%async_computation.8 | async-start | bytes 8912896 | tf_op jit(solution)/shard_map/reduce_scatter | solution.py:88
  324.9 6.3 %copy-start.2 = (bf16[2,512,4096]{2,1,0:T(8,128)(2,1)S(1)}, bf16[2,512,4096]{2,1,0:T(8,128)(2,1)}, u32[]{:S(2)}) copy-start(bf16[2,512,4096]{2,1,0:T(8,128)(2,1)} %reshape_reshape.3) | copy-start | bytes 25165828
  324.9 6.3 %copy-start.3 = (bf16[2,96,4096]{2,1,0:T(8,128)(2,1)S(1)}, bf16[2,96,4096]{2,1,0:T(8,128)(2,1)}, u32[]{:S(2)}) copy-start(bf16[2,96,4096]{2,1,0:T(8,128)(2,1)} %param.12) | copy-start | bytes 4718596
  333.9 11.3 %copy-start.5 = (bf16[2,96,4096]{2,1,0:T(8,128)(2,1)S(1)}, bf16[2,96,4096]{2,1,0:T(8,128)(2,1)}, u32[]{:S(2)}) copy-start(bf16[2,96,4096]{2,1,0:T(8,128)(2,1)} %param.13) | copy-start | bytes 4718596
  351.4 8.4 %copy-start.4 = (bf16[2,96,4096]{2,1,0:T(8,128)(2,1)S(1)}, bf16[2,96,4096]{2,1,0:T(8,128)(2,1)}, u32[]{:S(2)}) copy-start(bf16[2,96,4096]{2,1,0:T(8,128)(2,1)} %param.12) | copy-start | bytes 4718596
  429.6 24.1 %all-to-all-start.5 = ((f32[2,16,2]{2,0,1:T(2,128)}), f32[2,16,2]{2,0,1:T(2,128)S(1)}, u32[]{:S(2)}, u32[]{:S(2)}) async-start(f32[2,16,2]{2,0,1:T(2,128)} %copy.101), calls=%async_computation.6 | async-start | bytes 32768 | tf_op jit(solution)/shard_map/all_to_all | solution.py:99
  453.6 15.8 %all-to-all-start.4 = ((bf16[2,16,2,4096]{3,2,0,1:T(2,128)(2,1)}), bf16[2,16,2,4096]{3,2,0,1:T(2,128)(2,1)S(1)}, u32[]{:S(2)}, u32[]{:S(2)}) async-start(bf16[2,16,2,4096]{3,2,0,1:T(2,128)(2,1)} %copy.99), calls=%async_computation.5 | async-start | bytes 1048576 | tf_op jit(solution)/shard_map/all_to_all | solution.py:91
  460.7 10.2 %copy-start.1 = (bf16[2,96,4096]{2,1,0:T(8,128)(2,1)S(1)}, bf16[2,96,4096]{2,1,0:T(8,128)(2,1)}, u32[]{:S(2)}) copy-start(bf16[2,96,4096]{2,1,0:T(8,128)(2,1)} %param.11) | copy-start | bytes 4718596
Sparse Core Ops, SparseCore 0:
  71.7 167.5 all-gather.1
  382.6 68.5 reduce-scatter.1
